TPU v7x, 128 devices: a whole 4x4x4 slice. The times are simulated.
128 devices in a mesh: row: 64 (over y, x, z_lo, core), col: 2 (over z_hi).
Axes of the slice: x: 4, y: 4, z: 4 (z_hi: 2, z_lo: 2; z = z_hi * 2 + z_lo), core: 2. Of those that a mesh axis runs over, the one named last changes fastest.
Arguments:
- dist_first: bfloat16 [32768, 32768], P('row', 'col'), may hold values from -0.34 to 0.34
- coupling: bfloat16 [32768, 256], P('row', 'col'), may hold values from 0.099609375 to 1
- dist_second: bfloat16 [256, 512], P(None, 'col'), may hold values from -12 to 12
- row_potential: float32 [32768], P('row'), may hold values from -150 to 120
- column_cost: float32 [512], P('col'), may hold values from -300 to 20
- column_mass: float32 [512], P('col'), may hold values from 0.5 to 2
Outputs:
- transport: bfloat16 [32768, 512], P('row', 'col')
- potential: float32 [512], P('col')
All inputs are finite; a program needn't handle non-finite values.
Results may differ from a plain program's by a relative error of at most 0.0051.
Values may be sent and summed in bfloat16 or wider, within the bound.
No kernel may reach another device: no remote copies, remote signals or barrier semaphores. Data moves between devices by JAX's collectives and lax.ppermute only.
A program may use at most 128 MiB of HBM per device.

v0:
```python
import jax
import jax.numpy as jnp
from jax import lax
from jax.sharding import PartitionSpec as P

N = 32768


def joined_along(blocks, dim):
    shape = list(blocks.shape[1:])
    shape[dim] *= blocks.shape[0]
    return jnp.moveaxis(blocks, 0, dim).reshape(shape)


def copy_for_each(array, axis):
    copies = jnp.broadcast_to(array, (lax.axis_size(axis), *array.shape))
    return lax.all_to_all(copies, axis, split_axis=0, concat_axis=0, tiled=True)


def gather_directly(array, axis, dim):
    return joined_along(copy_for_each(array, axis), dim)


def split_up(array, dim, length):
    shape = array.shape
    blocks = array.reshape(*shape[:dim], length, shape[dim] // length, *shape[dim + 1 :])
    return jnp.moveaxis(blocks, dim, 0)


def summed_on_arrival(array, axis, dim):
    length = lax.axis_size(axis)
    blocks = lax.all_to_all(split_up(array, dim, length), axis, 0, 0, tiled=True)
    return jnp.sum(blocks, axis=0)


def all_in_one(array, axis):
    leaves = jax.tree.leaves(array)
    sequence = sorted(range(len(leaves)), key=lambda k: -leaves[k].size)
    width = (1, *leaves[sequence[0]].shape)[-1]
    lines = [
        jnp.pad(leaves[k].reshape(-1), (0, -leaves[k].size % width)).reshape(-1, width)
        for k in sequence
    ]
    both, at, found = (copy_for_each(jnp.concatenate(lines), axis), 0, {})
    for k, line in zip(sequence, lines):
        section = both[:, at : at + len(line)].reshape(len(both), -1)
        found[k] = section[:, : leaves[k].size].reshape(-1, *leaves[k].shape)
        at += len(line)
    numbers = iter(range(len(leaves)))
    return jax.tree.map(lambda _: found[next(numbers)], array)


def combined_pairwise(pieces, combine):
    while len(jax.tree.leaves(pieces)[0]) > 1:
        pieces = jax.vmap(combine)(
            *(jax.tree.map(lambda part: part[side::2], pieces) for side in (0, 1))
        )
    return jax.tree.map(lambda part: part[0], pieces)


def merged(array, axis, combine):
    pieces = all_in_one(array, axis)
    return combined_pairwise(pieces, combine)


def merge_columns(earlier, later):
    highest = jnp.maximum(earlier[0], later[0])
    summed = earlier[1] * jnp.exp(earlier[0] - highest) + later[1] * jnp.exp(later[0] - highest)
    return (highest, summed)


def body(dist_first, coupling, dist_second, row_potential, column_cost, column_mass):
    groups = lax.axis_size("col")
    stacked = lax.all_gather(coupling, "row", axis=0, tiled=True)
    total_rows = stacked.shape[0]
    stacked = stacked.reshape(groups, 1, total_rows // groups, stacked.shape[1])
    traded = lax.all_to_all(stacked, "col", split_axis=0, concat_axis=1, tiled=True)
    second_full = gather_directly(dist_second, "col", 1)
    second_blocks = second_full.reshape(
        groups, second_full.shape[0] // groups, second_full.shape[1]
    )
    product = jnp.einsum(
        "jnk,jkq->nq", traded[0], second_blocks, preferred_element_type=jnp.float32
    ).astype(jnp.bfloat16)
    partial_value = jnp.dot(dist_first, product, preferred_element_type=jnp.float32)
    gradient = summed_on_arrival(partial_value, "col", 1)
    scores = row_potential[:, None] + 2.0 * gradient - column_cost[None, :]
    local_high = jnp.max(scores, axis=0)
    local_sum = jnp.sum(jnp.exp(scores - local_high[None, :]), axis=0)
    highest, column_sum = merged((local_high, local_sum), "row", merge_columns)
    weights = jnp.exp(scores - highest[None, :])
    potential = jnp.log(column_mass) - highest - jnp.log(column_sum)
    transport = (weights * (N * column_mass / column_sum)[None, :]).astype(jnp.bfloat16)
    return (transport, potential)


def solution(mesh):
    in_specs = (P("row", "col"), P("row", "col"), P(None, "col"), P("row"), P("col"), P("col"))
    out_specs = (P("row", "col"), P("col"))
    return jax.shard_map(body, mesh=mesh, in_specs=in_specs, out_specs=out_specs, check_vma=False)
```

profile of v0, /device:TPU:1, one launch (start us, length us, event | category | flops | bytes accessed | tf_op | source)
XLA Modules:
  0.0 284.0 jit_solution(13788722296052831946)
XLA Ops:
  7.2 0.0 all-gather.2.cloned.1.call-start
  7.2 0.7 all-gather.2.cloned.1.call-update
  7.9 0.9 broadcast_in_dim.4
  8.8 11.0 %all_to_all.24 = bf16[2,256,256]{2,1,0:T(8,128)(2,1)S(1)} all-to-all(bf16[2,256,256]{2,1,0:T(8,128)(2,1)S(1)} %broadcast_in_dim.4), channel_id=1, replica_groups=mesh['row'=64,'col'=2] {'col'}, dimensions={0} | all-to-all | bytes 524288 | tf_op jit(solution)/shard_map/all_to_all | solution.py:17
  19.8 104.5 %all-gather.2.cloned.1.call-done = bf16[32768,128]{1,0:T(8,128)(2,1)} async-done(((bf16[512,128]{1,0:T(8,128)(2,1)}), bf16[32768,128]{1,0:T(8,128)(2,1)}) %all-gather.2.cloned.1.call-update) | async-done | bytes 8388624 | tf_op jit(solution)/shard_map/all_gather | solution.py:74
  124.4 6.9 %all-to-all-start = ((bf16[2,1,16384,128]{3,2,1,0:T(8,128)(2,1)}), bf16[2,1,16384,128]{3,2,1,0:T(8,128)(2,1)}, u32[]{:S(2)}, u32[]{:S(2)}) async-start(bf16[2,1,16384,128]{3,2,1,0:T(8,128)(2,1)} %bitcast.26), calls=%async_computation | async-start | bytes 16777216 | tf_op jit(solution)/shard_map/all_to_all | solution.py:77
  131.3 0.3 copy.10
  131.6 0.2 reshape_reshape.3
  131.8 0.0 copy-start
  131.8 0.0 copy-start.1
  131.8 0.0 copy-start.2
  131.8 93.2 %all-to-all-done = bf16[2,1,16384,128]{3,2,1,0:T(8,128)(2,1)} async-done(((bf16[2,1,16384,128]{3,2,1,0:T(8,128)(2,1)}), bf16[2,1,16384,128]{3,2,1,0:T(8,128)(2,1)}, u32[]{:S(2)}, u32[]{:S(2)}) %all-to-all-start) | async-done | bytes 8388640 | tf_op jit(solution)/shard_map/all_to_all | solution.py:77
  225.0 16.6 %fusion.2 = f32[512,512]{1,0:T(8,128)S(1)} fusion(bf16[512,16384]{1,0:T(8,128)(2,1)} %param.6, bf16[2,128,512]{2,1,0:T(8,128)(2,1)S(1)} %reshape_reshape.3, bf16[2,1,16384,128]{3,2,1,0:T(8,128)(2,1)} %all-to-all-done), kind=kOutput, calls=%fused_computation.2 | convolution fusion | flops 12893290496 | bytes 26476544 | tf_op jit(solution)/shard_map/dot_general | solution.py:85
  241.6 16.5 %all_to_all.25 = f32[2,512,256]{1,2,0:T(8,128)S(1)} all-to-all(f32[2,512,256]{1,2,0:T(8,128)S(1)} %bitcast.27), channel_id=1, replica_groups=mesh['row'=64,'col'=2] {'col'}, dimensions={0} | all-to-all | bytes 2097152 | tf_op jit(solution)/shard_map/all_to_all | solution.py:32
  258.1 0.1 reduce_sum.18
  258.2 0.0 copy-done
  258.2 0.0 copy-done.1
  258.2 0.2 fusion.4
  258.4 0.2 exponential_reduce_fusion
  258.7 16.2 %all_to_all.26 = f32[64,2,256]{2,1,0:T(2,128)S(1)} all-to-all(f32[64,2,256]{2,1,0:T(2,128)S(1)} %broadcast_in_dim.5), channel_id=1, replica_groups=mesh['row'=64,'col'=2] {'row'}, dimensions={0} | all-to-all | bytes 262144 | tf_op jit(solution)/shard_map/all_to_all | solution.py:17
  274.9 0.1 fusion.6
  275.6 0.0 copy-done.2
  275.6 0.6 log_subtract_fusion
  276.2 0.2 multiply_convert_fusion
  276.4 0.8 copy.12
  (29 shorter events, 0.5 us)
Async XLA Ops:
  7.2 117.2 %all-gather.2.cloned.1.call-start = ((), (), s32[]{:S(2)}) async-start(), calls=%async_computation.4 | async-start | bytes 8519680 | tf_op jit(solution)/shard_map/all_gather | solution.py:74
  124.4 100.6 %all-to-all-start = ((bf16[2,1,16384,128]{3,2,1,0:T(8,128)(2,1)}), bf16[2,1,16384,128]{3,2,1,0:T(8,128)(2,1)}, u32[]{:S(2)}, u32[]{:S(2)}) async-start(bf16[2,1,16384,128]{3,2,1,0:T(8,128)(2,1)} %bitcast.26), calls=%async_computation | async-start | bytes 16777216 | tf_op jit(solution)/shard_map/all_to_all | solution.py:77
  131.8 126.4 %copy-start = (f32[512]{0:T(512)S(1)}, f32[512]{0:T(512)}, u32[]{:S(2)}) copy-start(f32[512]{0:T(512)} %param.9) | copy-start | bytes 6148
  131.8 126.4 %copy-start.1 = (f32[256]{0:T(256)S(1)}, f32[256]{0:T(256)}, u32[]{:S(2)}) copy-start(f32[256]{0:T(256)} %param.10) | copy-start | bytes 3076
  131.8 143.8 %copy-start.2 = (f32[256]{0:T(256)S(1)}, f32[256]{0:T(256)}, u32[]{:S(2)}) copy-start(f32[256]{0:T(256)} %param.11) | copy-start | bytes 3076
Sparse Core Ops, SparseCore 0:
  9.7 114.6 all-gather.1
where the time goes:
time: 284 us
  waiting for transfers between devices  198 us (70%)
  blocking collectives  43.7 us (15%)
  matrix products  16.6 us (6%)
  between operations  14.2 us (5%)
  starting transfers between devices  6.97 us (2%)
    all_gather x1, waiting for transfers between devices, body(): stacked = lax.all_gather(coupling, 'row', axis=0, tiled=True)  105 us
    all_to_all x1, waiting for transfers between devices, body(): lax.all_to_all(stacked, 'col', split_axis=0, concat_axis=1, tiled=True)  93.2 us
    all_to_all x2, blocking collectives, copy_for_each(): return lax.all_to_all(copies, axis, split_axis=0, concat_axis=0, tiled=True)  27.2 us
    dot_general x1, matrix products, body(): jnp.dot(dist_first, product, preferred_element_type=jnp.float32)  16.6 us
    all_to_all x1, blocking collectives, summed_on_arrival(): lax.all_to_all(split_up(array, dim, length), axis, 0, 0, tiled=True)  16.5 us
    all_to_all x1, starting transfers between devices, body(): lax.all_to_all(stacked, 'col', split_axis=0, concat_axis=1, tiled=True)  6.93 us
  transfers between devices with their start and end apart: 2, of which 2 were waited for; matrix products, arithmetic and copies ran while one was open for 0% of the time, Pallas kernels for 0%

commit v1 on v0

--- a/solution.py
+++ b/solution.py
@@ -71,7 +71,9 @@
 
 def body(dist_first, coupling, dist_second, row_potential, column_cost, column_mass):
     groups = lax.axis_size("col")
-    stacked = lax.all_gather(coupling, "row", axis=0, tiled=True)
+    stacked = jnp.concatenate(
+        lax.all_to_all(jnp.stack([coupling] * lax.axis_size("row")), "row", 0, 0), axis=0
+    )
     total_rows = stacked.shape[0]
     stacked = stacked.reshape(groups, 1, total_rows // groups, stacked.shape[1])
     traded = lax.all_to_all(stacked, "col", split_axis=0, concat_axis=1, tiled=True)

time: 284 us -> 274 us (0.965)
  blocking collectives: 43.7 us -> 149 us
  waiting for transfers between devices: 198 us -> 93.3 us
  between operations: 14.2 us -> 0.81 us
  local copies, waits for them, and re-layouts: 2.76 us -> 5.67 us
    all_to_all x0 -> x1, blocking collectives: none -> 106 us  [body(): lax.all_to_all(jnp.stack([coupling] * lax.axis_size('row')), 'row', 0, 0)]
    all_gather x1 -> x0, waiting for transfers between devices: 105 us -> none  [body(): stacked = lax.all_gather(coupling, 'row', axis=0, tiled=True)]
    another operation x0 -> x1, local copies, waits for them, and re-layouts: none -> 2.91 us  [body(): jnp.stack([coupling] * lax.axis_size('row'))]
  transfers between devices with their start and end apart: 2 -> 1, of which waited for: 2 -> 1; matrix products, arithmetic and copies ran while one was open for 0% -> 0% of each run, Pallas kernels for 0% -> 0%
where the time goes in v1:
time: 274 us
  blocking collectives  149 us (54%)
  waiting for transfers between devices  93.3 us (34%)
  matrix products  16.6 us (6%)
  starting transfers between devices  6.93 us (3%)
  local copies, waits for them, and re-layouts  5.67 us (2%)
    all_to_all x1, blocking collectives, body(): lax.all_to_all(jnp.stack([coupling] * lax.axis_size('row')), 'row', 0, 0)  106 us
    all_to_all x1, waiting for transfers between devices, body(): lax.all_to_all(stacked, 'col', split_axis=0, concat_axis=1, tiled=True)  93.3 us
    all_to_all x2, blocking collectives, copy_for_each(): return lax.all_to_all(copies, axis, split_axis=0, concat_axis=0, tiled=True)  25.9 us
    all_to_all x1, blocking collectives, summed_on_arrival(): lax.all_to_all(split_up(array, dim, length), axis, 0, 0, tiled=True)  16.6 us
    dot_general x1, matrix products, body(): jnp.dot(dist_first, product, preferred_element_type=jnp.float32)  16.6 us
    all_to_all x1, starting transfers between devices, body(): lax.all_to_all(stacked, 'col', split_axis=0, concat_axis=1, tiled=True)  6.93 us
  transfers between devices with their start and end apart: 1, of which 1 were waited for; matrix products, arithmetic and copies ran while one was open for 0% of the time, Pallas kernels for 0%

profile of v1, /device:TPU:1, one launch (start us, length us, event | category | flops | bytes accessed | tf_op | source)
XLA Modules:
  0.0 273.5 jit_solution(5199391143547492866)
XLA Ops:
  0.6 0.9 broadcast_in_dim.4
  1.6 11.0 %all_to_all.29 = bf16[2,256,256]{2,1,0:T(8,128)(2,1)S(1)} all-to-all(bf16[2,256,256]{2,1,0:T(8,128)(2,1)S(1)} %broadcast_in_dim.4), channel_id=1, replica_groups=mesh['row'=64,'col'=2] {'col'}, dimensions={0} | all-to-all | bytes 524288 | tf_op jit(solution)/shard_map/all_to_all | solution.py:17
  12.6 2.9 %stack.2 = bf16[64,512,128]{2,1,0:T(8,128)(2,1)S(1)} broadcast(bf16[512,128]{1,0:T(8,128)(2,1)} %param.7), dimensions={1,2} | broadcast | bytes 8519680 | tf_op jit(solution)/shard_map/stack | solution.py:75
  15.5 106.4 %all_to_all.30 = bf16[64,512,128]{2,1,0:T(8,128)(2,1)} all-to-all(bf16[64,512,128]{2,1,0:T(8,128)(2,1)S(1)} %stack.2), channel_id=1, replica_groups=mesh['row'=64,'col'=2] {'row'}, dimensions={0} | all-to-all | bytes 16777216 | tf_op jit(solution)/shard_map/all_to_all | solution.py:75
  121.9 6.9 %all-to-all-start.1 = ((bf16[2,1,16384,128]{3,2,1,0:T(8,128)(2,1)}), bf16[2,1,16384,128]{3,2,1,0:T(8,128)(2,1)}, u32[]{:S(2)}, u32[]{:S(2)}) async-start(bf16[2,1,16384,128]{3,2,1,0:T(8,128)(2,1)} %bitcast.26), calls=%async_computation.1 | async-start | bytes 16777216 | tf_op jit(solution)/shard_map/all_to_all | solution.py:79
  128.8 0.3 copy.10
  129.1 0.2 reshape_reshape.7
  129.3 0.0 copy-start
  129.3 0.0 copy-start.1
  129.3 0.0 copy-start.2
  129.3 93.3 %all-to-all-done.1 = bf16[2,1,16384,128]{3,2,1,0:T(8,128)(2,1)} async-done(((bf16[2,1,16384,128]{3,2,1,0:T(8,128)(2,1)}), bf16[2,1,16384,128]{3,2,1,0:T(8,128)(2,1)}, u32[]{:S(2)}, u32[]{:S(2)}) %all-to-all-start.1) | async-done | bytes 8388640 | tf_op jit(solution)/shard_map/all_to_all | solution.py:79
  222.6 16.6 %fusion.2 = f32[512,512]{1,0:T(8,128)S(1)} fusion(bf16[512,16384]{1,0:T(8,128)(2,1)} %param.6, bf16[2,128,512]{2,1,0:T(8,128)(2,1)S(1)} %reshape_reshape.7, bf16[2,1,16384,128]{3,2,1,0:T(8,128)(2,1)} %all-to-all-done.1), kind=kOutput, calls=%fused_computation.2 | convolution fusion | flops 12893290496 | bytes 26476544 | tf_op jit(solution)/shard_map/dot_general | solution.py:87
  239.2 16.6 %all_to_all.31 = f32[2,512,256]{1,2,0:T(8,128)S(1)} all-to-all(f32[2,512,256]{1,2,0:T(8,128)S(1)} %bitcast.27), channel_id=1, replica_groups=mesh['row'=64,'col'=2] {'col'}, dimensions={0} | all-to-all | bytes 2097152 | tf_op jit(solution)/shard_map/all_to_all | solution.py:32
  255.8 0.1 reduce_sum.18
  255.9 0.0 copy-done
  255.9 0.0 copy-done.1
  255.9 0.2 fusion.4
  256.1 0.2 exponential_reduce_fusion
  256.4 14.8 %all_to_all.32 = f32[64,2,256]{2,1,0:T(2,128)S(1)} all-to-all(f32[64,2,256]{2,1,0:T(2,128)S(1)} %broadcast_in_dim.5), channel_id=1, replica_groups=mesh['row'=64,'col'=2] {'row'}, dimensions={0} | all-to-all | bytes 262144 | tf_op jit(solution)/shard_map/all_to_all | solution.py:17
  271.2 0.1 fusion.6
  271.9 0.0 copy-done.2
  271.9 0.6 log_subtract_fusion
  272.5 0.2 multiply_convert_fusion
  272.7 0.8 copy.12
  (29 shorter events, 0.5 us)
Async XLA Ops:
  121.9 100.7 %all-to-all-start.1 = ((bf16[2,1,16384,128]{3,2,1,0:T(8,128)(2,1)}), bf16[2,1,16384,128]{3,2,1,0:T(8,128)(2,1)}, u32[]{:S(2)}, u32[]{:S(2)}) async-start(bf16[2,1,16384,128]{3,2,1,0:T(8,128)(2,1)} %bitcast.26), calls=%async_computation.1 | async-start | bytes 16777216 | tf_op jit(solution)/shard_map/all_to_all | solution.py:79
  129.3 126.6 %copy-start = (f32[512]{0:T(512)S(1)}, f32[512]{0:T(512)}, u32[]{:S(2)}) copy-start(f32[512]{0:T(512)} %param.9) | copy-start | bytes 6148
  129.3 126.6 %copy-start.1 = (f32[256]{0:T(256)S(1)}, f32[256]{0:T(256)}, u32[]{:S(2)}) copy-start(f32[256]{0:T(256)} %param.10) | copy-start | bytes 3076
  129.3 142.6 %copy-start.2 = (f32[256]{0:T(256)S(1)}, f32[256]{0:T(256)}, u32[]{:S(2)}) copy-start(f32[256]{0:T(256)} %param.11) | copy-start | bytes 3076
